TPU v7x, 256 devices: a whole 4x4x8 slice. The times are simulated.
256 devices in a mesh: tm: 128 (over z, y_lo, x, core), net: 2 (over y_hi).
Axes of the slice: x: 4, y: 4 (y_hi: 2, y_lo: 2; y = y_hi * 2 + y_lo), z: 8, core: 2. Of those that a mesh axis runs over, the one named last changes fastest.
Arguments:
- direction_nodal: float32 [1, 128, 2, 8192], P(None, 'tm', None, 'net'), may hold values from -27 to 27
- direction_capacity: float32 [1, 128, 65536], P(None, 'tm', 'net'), may hold values from -27 to 27
- residual_nodal: float32 [1, 128, 2, 8192], P(None, 'tm', None, 'net'), may hold values from -27 to 27
- residual_capacity: float32 [1, 128, 65536], P(None, 'tm', 'net'), may hold values from -27 to 27
- scale_flow: float32 [128, 12288], P('tm', 'net'), may hold values from 0.25 to 4
- scale_dispatch: float32 [128, 65536], P('tm', 'net'), may hold values from 0.25 to 4
- scale_storage: float32 [128, 2, 8192], P('tm', None, 'net'), may hold values from 0.25 to 4
- scale_capacity: float32 [65536], P('net'), may hold values from 0.02 to 0.3
- availability: float32 [128, 65536], P('tm', 'net'), may hold values from 0.05 to 1
- retention: float32 [8192], P('net'), may hold values from 0.5 to 1
- line_anchor: int32 [96], P('net'), may hold values from 0 to 63
- line_target: int32 [96], P('net'), may hold values from 0 to 63
- anchor_rows: int32 [12288], P('net'), may hold values from 0 to 127
- target_rows: int32 [12288], P('net'), may hold values from 0 to 127
- column_block: int32 [512], P('net'), may hold values from 0 to 63
- column_rows: int32 [65536], P('net'), may hold values from 0 to 127
Outputs:
- updated_nodal: float32 [1, 128, 2, 8192], P(None, 'tm', None, 'net')
- updated_capacity: float32 [1, 128, 65536], P(None, 'tm', 'net')
All inputs are finite; a program needn't handle non-finite values.
Results may differ from a plain program's by a relative error of at most 0.00002.
Values sent between devices are 32-bit elements; how exact they have to be, the bound alone decides.
No kernel may reach another device: no remote copies, remote signals or barrier semaphores. Data moves between devices by JAX's collectives and lax.ppermute only.
A program may use at most 64 MiB of HBM per device.

v0:
```python
import jax
import jax.numpy as jnp
from jax import lax
from jax.sharding import PartitionSpec as P

BLOCK = 128
DAMPING = 0.5


def passed_along(value, axis, steps):
    count = lax.axis_size(axis)
    pairs = [(source, (source + steps) % count) for source in range(count)]
    return lax.ppermute(value, axis, pairs)


def body(
    direction_nodal,
    direction_capacity,
    residual_nodal,
    residual_capacity,
    scale_flow,
    scale_dispatch,
    scale_storage,
    scale_capacity,
    availability,
    retention,
    line_anchor,
    line_target,
    anchor_rows,
    target_rows,
    column_block,
    column_rows,
):
    anchor = jnp.repeat(line_anchor, BLOCK) * BLOCK + anchor_rows
    target = jnp.repeat(line_target, BLOCK) * BLOCK + target_rows
    column_bus = jnp.repeat(column_block, BLOCK) * BLOCK + column_rows
    balance = direction_nodal[:, :, 0, :]
    storage = direction_nodal[:, :, 1, :]
    network = lax.all_gather(balance, "net", axis=2, tiled=True)
    next_first = passed_along(storage, "tm", -1)
    storage_next = jnp.concatenate([storage[:, 1:, :], next_first], axis=1)
    flow_value = jnp.take(network, anchor, axis=2) - jnp.take(network, target, axis=2)
    dispatch_value = jnp.take(network, column_bus, axis=2) + direction_capacity
    partial_sums = -jnp.sum(availability[None] * direction_capacity, axis=1)
    level_value = storage - retention * storage_next
    charge_value = balance - storage
    flow_scaled = scale_flow[None] * flow_value
    dispatch_scaled = scale_dispatch[None] * dispatch_value
    level_scaled = scale_storage[None, :, 0, :] * level_value
    charge_scaled = scale_storage[None, :, 1, :] * charge_value
    capacity_value = lax.psum(partial_sums, "tm")
    capacity_scaled = scale_capacity[None] * capacity_value
    squares_local = jnp.sum(residual_nodal * residual_nodal, axis=(1, 2, 3)) + jnp.sum(
        residual_capacity * residual_capacity, axis=(1, 2)
    )
    bus_terms = jnp.zeros(network.shape, jnp.float32).at[:, :, anchor].add(flow_scaled)
    bus_terms = (
        bus_terms.at[:, :, target].add(-flow_scaled).at[:, :, column_bus].add(dispatch_scaled)
    )
    own_terms = lax.psum_scatter(bus_terms, "net", scatter_dimension=2, tiled=True)
    image_balance = own_terms + charge_scaled + DAMPING * balance
    behind = passed_along(level_scaled, "tm", 1)
    level_before = jnp.concatenate([behind, level_scaled[:, :-1, :]], axis=1)
    image_storage = level_scaled - retention * level_before - charge_scaled + DAMPING * storage
    image_limit = (
        dispatch_scaled
        - availability[None] * capacity_scaled[:, None, :]
        + DAMPING * direction_capacity
    )
    image_nodal = jnp.stack([image_balance, image_storage], axis=2)
    curvature_local = jnp.sum(direction_nodal * image_nodal, axis=(1, 2, 3)) + jnp.sum(
        direction_capacity * image_limit, axis=(1, 2)
    )
    squares, curvature = lax.psum((squares_local, curvature_local), ("tm", "net"))
    step_size = squares / curvature
    updated_nodal = residual_nodal - step_size[:, None, None, None] * image_nodal
    updated_capacity = residual_capacity - step_size[:, None, None] * image_limit
    return (updated_nodal, updated_capacity)


def solution(mesh):
    in_specs = (
        P(None, "tm", None, "net"),
        P(None, "tm", "net"),
        P(None, "tm", None, "net"),
        P(None, "tm", "net"),
        P("tm", "net"),
        P("tm", "net"),
        P("tm", None, "net"),
        P("net"),
        P("tm", "net"),
        P("net"),
        P("net"),
        P("net"),
        P("net"),
        P("net"),
        P("net"),
        P("net"),
    )
    out_specs = (P(None, "tm", None, "net"), P(None, "tm", "net"))
    return jax.shard_map(body, mesh=mesh, in_specs=in_specs, out_specs=out_specs, check_vma=False)
```

profile of v0, /device:TPU:1, one launch (start us, length us, event | category | flops | bytes accessed | tf_op | source)
XLA Modules:
  0.0 1337.2 jit_solution(10901547301141026485)
XLA Ops:
  7.2 0.0 all-reduce.3.cloned.1.call-start
  7.2 1.8 fusion.3
  9.0 0.0 all-reduce.3.cloned.1.call-update
  9.0 0.0 reduce-scatter.4.cloned.1.call-start
  9.1 0.9 fusion.11
  9.9 3.3 collective-permute-start
  13.3 4.8 all-gather
  18.0 0.7 broadcast_multiply_fusion.1
  18.7 0.7 broadcast_multiply_fusion.2
  19.3 0.8 broadcast_clamp_fusion.1
  20.2 34.3 %gather_fusion.2 = f32[6144]{0:T(1024)S(1)} fusion(f32[8192]{0:T(1024)S(1)} %bitcast.85, s32[6144]{0:T(1024)S(1)} %get-tuple-element.12), kind=kCustom, calls=%fused_computation.1.clone | custom fusion | bytes 73728 | tf_op jit(solution)/shard_map/jit(_take)/gather | solution.py:42
  54.5 0.1 broadcast_clamp_fusion.2
  54.6 34.3 %gather_fusion.1 = f32[6144]{0:T(1024)S(1)} fusion(f32[8192]{0:T(1024)S(1)} %bitcast.86, s32[6144]{0:T(1024)S(1)} %get-tuple-element.14), kind=kCustom, calls=%fused_computation.clone | custom fusion | bytes 73728 | tf_op jit(solution)/shard_map/jit(_take)/gather | solution.py:42
  88.9 0.1 broadcast_clamp_fusion
  89.0 180.5 %gather_fusion = f32[32768]{0:T(1024)S(1)} fusion(f32[8192]{0:T(1024)S(1)} %bitcast.87, s32[32768]{0:T(1024)S(1)} %get-tuple-element.8), kind=kCustom, calls=%fused_computation.2 | custom fusion | bytes 393216 | tf_op jit(solution)/shard_map/jit(_take)/gather | solution.py:43
  269.7 0.1 fusion.10
  269.7 0.9 multiply_reduce_fusion.1
  270.6 42.8 %scatter_custom_fusion = f32[8192]{0:T(1024)S(1)} fusion(s32[6144]{0:T(1024)S(1)} %get-tuple-element.15, f32[6144]{0:T(1024)S(1)} %bitcast.99, f32[]{:T(128)} %constant.15.clone.1), kind=kCustom, calls=%fused_computation.36 | custom fusion | flops 6144 | bytes 32772 | tf_op jit(solution)/shard_map/scatter-add | solution.py:56
  313.5 42.9 %scatter_fusion = f32[8192]{0:T(1024)S(1)} fusion(f32[8192]{0:T(1024)S(1)} %scatter_custom_fusion, s32[6144]{0:T(1024)S(1)} %get-tuple-element.13, f32[6144]{0:T(1024)S(1)} %bitcast.94), kind=kCustom, calls=%fused_computation.4 | custom fusion | flops 6144 | bytes 98304 | tf_op jit(solution)/shard_map/scatter-add | solution.py:58
  356.5 0.6 collective-permute-start.1
  357.1 593.0 %all-reduce.3.cloned.1.call-done = f32[1,32768]{1,0:T(1,128)} async-done(((f32[1,32768]{1,0:T(1,128)}), f32[1,32768]{1,0:T(1,128)}) %all-reduce.3.cloned.1.call-update) | async-done | bytes 131088 | tf_op jit(solution)/shard_map/psum | solution.py:51
  950.2 1.9 multiply_reduce_fusion
  952.1 225.9 %scatter_fusion.1 = f32[8192]{0:T(1024)S(1)} fusion(f32[8192]{0:T(1024)S(1)} %scatter_fusion, s32[32768]{0:T(1024)S(1)} %get-tuple-element.9, f32[32768]{0:T(1024)S(1)} %bitcast.91), kind=kCustom, calls=%fused_computation.5 | custom fusion | flops 32768 | bytes 524288 | tf_op jit(solution)/shard_map/scatter-add | solution.py:58
  1178.1 6.4 copy.18
  1184.5 0.6 multiply_reduce_fusion.3
  1186.3 57.5 %reduce-scatter.4.cloned.1.call-done = f32[4096,1]{1,0:T(8,128)} async-done(((f32[8192,1]{1,0:T(8,128)}), f32[4096,1]{1,0:T(8,128)}) %reduce-scatter.4.cloned.1.call-update) | async-done | bytes 16400
  1243.8 4.4 copy.19
  1248.3 0.1 fusion.5
  1248.4 0.7 multiply_reduce_fusion.2
  1250.4 77.2 %all-reduce = (f32[1]{0:T(128)}, f32[1]{0:T(128)}) all-reduce(f32[1]{0:T(128)} %bitcast.2, f32[1]{0:T(128)} %bitcast.31), channel_id=1, replica_groups=mesh['tm'=128,'net'=2] {'tm','net'}, use_global_device_ids=true, to_apply=%region_2.3 | all-reduce | flops 2 | bytes 16 | tf_op jit(solution)/shard_map/psum | solution.py:74
  1328.9 0.7 multiply_subtract_fusion.1
  1329.6 0.8 multiply_subtract_fusion
  (34 shorter events, 0.2 us)
Async XLA Ops:
  7.2 943.0 %all-reduce.3.cloned.1.call-start = ((), (), s32[]{:S(2)}) async-start(), calls=%async_computation.1 | async-start | bytes 262144 | tf_op jit(solution)/shard_map/psum | solution.py:51
  9.0 1234.8 %reduce-scatter.4.cloned.1.call-start = ((), (), s32[]{:S(2)}) async-start(), calls=%async_computation.2 | async-start | bytes 6291456
  9.9 346.5 %collective-permute-start = (f32[1,1,4096]{2,1,0:T(1,128)S(1)}, f32[1,1,4096]{2,1,0:T(1,128)S(1)}, u32[]{:S(2)}, u32[]{:S(2)}) collective-permute-start(f32[1,1,4096]{2,1,0:T(1,128)S(1)} %get-tuple-element.19), channel_id=1, source_target_pairs={{0,254},{2,0},{4,2},{6,4},{8,6},{10,8},{12,10},{14,12},{16,14},{18... | collective-permute-start | bytes 49160 | tf_op jit(solution)/shard_map/ppermute | solution.py:13
  20.2 34.3 %copy-start.10 = (s32[6144]{0:T(1024)S(1)}, s32[6144]{0:T(1024)}, u32[]{:S(2)}) copy-start(s32[6144]{0:T(1024)} %param.30) | copy-start | bytes 73732
  54.6 34.3 %copy-start.12 = (s32[256]{0:T(256)S(1)}, s32[256]{0:T(256)}, u32[]{:S(2)}) copy-start(s32[256]{0:T(256)} %param.32) | copy-start | bytes 3076
  54.6 34.3 %copy-start.4 = (s32[32768]{0:T(1024)S(1)}, s32[32768]{0:T(1024)}, u32[]{:S(2)}) copy-start(s32[32768]{0:T(1024)} %param.33) | copy-start | bytes 393220
  89.0 180.6 %copy-start.11 = (f32[1,6144]{1,0:T(1,128)S(1)}, f32[1,6144]{1,0:T(1,128)}, u32[]{:S(2)}) copy-start(f32[1,6144]{1,0:T(1,128)} %param.22) | copy-start | bytes 73732
  89.0 180.7 %copy-start = (f32[1,1,32768]{2,1,0:T(1,128)S(1)}, f32[1,1,32768]{2,1,0:T(1,128)}, u32[]{:S(2)}) copy-start(f32[1,1,32768]{2,1,0:T(1,128)} %param.21) | copy-start | bytes 393220
  313.4 43.0 %copy-start.3 = (f32[1,1,2,4096]{3,2,1,0:T(2,128)S(1)}, f32[1,1,2,4096]{3,2,1,0:T(2,128)}, u32[]{:S(2)}) copy-start(f32[1,1,2,4096]{3,2,1,0:T(2,128)} %param.18) | copy-start | bytes 98308
  313.5 43.0 %copy-start.8 = (f32[4096]{0:T(1024)S(1)}, f32[4096]{0:T(1024)}, u32[]{:S(2)}) copy-start(f32[4096]{0:T(1024)} %param.27) | copy-start | bytes 49156
  313.5 43.0 %copy-start.9 = (f32[1,2,4096]{2,1,0:T(2,128)S(1)}, f32[1,2,4096]{2,1,0:T(2,128)}, u32[]{:S(2)}) copy-start(f32[1,2,4096]{2,1,0:T(2,128)} %param.24) | copy-start | bytes 98308
  313.5 636.7 %copy-start.1 = (f32[1,1,32768]{2,1,0:T(1,128)S(1)}, f32[1,1,32768]{2,1,0:T(1,128)}, u32[]{:S(2)}) copy-start(f32[1,1,32768]{2,1,0:T(1,128)} %param.19) | copy-start | bytes 393220
  313.5 636.7 %copy-start.2 = (f32[1,32768]{1,0:T(1,128)S(1)}, f32[1,32768]{1,0:T(1,128)}, u32[]{:S(2)}) copy-start(f32[1,32768]{1,0:T(1,128)} %param.26) | copy-start | bytes 393220
  313.5 636.7 %copy-start.6 = (f32[32768]{0:T(1024)S(1)}, f32[32768]{0:T(1024)}, u32[]{:S(2)}) copy-start(f32[32768]{0:T(1024)} %param.25) | copy-start | bytes 393220
  313.5 636.7 %copy-start.7 = (f32[1,32768]{1,0:T(1,128)S(1)}, f32[1,32768]{1,0:T(1,128)}, u32[]{:S(2)}) copy-start(f32[1,32768]{1,0:T(1,128)} %param.23) | copy-start | bytes 393220
  356.5 891.7 %collective-permute-start.1 = (f32[1,1,4096]{2,1,0:T(1,128)S(1)}, f32[1,1,4096]{2,1,0:T(1,128)S(1)}, u32[]{:S(2)}, u32[]{:S(2)}) collective-permute-start(f32[1,1,4096]{2,1,0:T(1,128)S(1)} %subtract_multiply_fusion), channel_id=1, source_target_pairs={{0,2},{2,4},{4,6},{6,8},{8,10},{10,12},{12,14},{14,16},{16,18},{18... | collective-permute-start | bytes 49160 | tf_op jit(solution)/shard_map/ppermute | solution.py:13
  1178.1 6.4 copy-start.5
Sparse Core Ops, SparseCore 0:
  11.2 938.9 all-reduce.2
  1184.6 59.2 reduce-scatter.3
where the time goes:
time: 1340 us
  waiting for transfers between devices  651 us (49%)
  other arithmetic  322 us (24%)
  local copies, waits for them, and re-layouts  261 us (19%)
  blocking collectives  81.9 us (6%)
  between operations  18.3 us (1%)
    psum x1, waiting for transfers between devices, body(): capacity_value = lax.psum(partial_sums, 'tm')  593 us
    scatter-add x2, other arithmetic, body(): bus_terms.at[:, :, target].add(-flow_scaled).at[:, :, column_bus]  269 us
    gather x1, local copies, waits for them, and re-layouts, body(): dispatch_value = jnp.take(network, column_bus, axis=2) + direction_capacity  181 us
    psum x1, blocking collectives, body(): lax.psum((squares_local, curvature_local), ('tm', 'net'))  77.2 us
    unnamed x3, waiting for transfers between devices  57.5 us
    scatter-add x1, other arithmetic, body(): jnp.zeros(network.shape, jnp.float32).at[:, :, anchor].add(flow_scaled)  42.8 us
    gather x1, local copies, waits for them, and re-layouts, body(): jnp.take(network, target, axis=2)  34.3 us
    gather x1, local copies, waits for them, and re-layouts, body(): jnp.take(network, anchor, axis=2) - jnp.take(network, target, axis=2)  34.3 us
  transfers between devices with their start and end apart: 4, of which 2 were waited for; matrix products, arithmetic and copies ran while one was open for 43% of the time, Pallas kernels for 0%

commit v1 on v0

--- a/solution.py
+++ b/solution.py
@@ -48,7 +48,7 @@
     dispatch_scaled = scale_dispatch[None] * dispatch_value
     level_scaled = scale_storage[None, :, 0, :] * level_value
     charge_scaled = scale_storage[None, :, 1, :] * charge_value
-    capacity_value = lax.psum(partial_sums, "tm")
+    capacity_value = jnp.sum(lax.all_gather(partial_sums, axis_name="tm"), axis=0)
     capacity_scaled = scale_capacity[None] * capacity_value
     squares_local = jnp.sum(residual_nodal * residual_nodal, axis=(1, 2, 3)) + jnp.sum(
         residual_capacity * residual_capacity, axis=(1, 2)

time: 1340 us -> 762 us (0.57)
  waiting for transfers between devices: 651 us -> 64.1 us
    psum x1 -> x0, waiting for transfers between devices: 593 us -> none  [body(): capacity_value = lax.psum(partial_sums, 'tm')]
  transfers between devices with their start and end apart: 4 -> 4, of which waited for: 2 -> 1; matrix products, arithmetic and copies ran while one was open for 43% -> 77% of each run, Pallas kernels for 0% -> 0%
where the time goes in v1:
time: 762 us
  other arithmetic  332 us (44%)
  local copies, waits for them, and re-layouts  261 us (34%)
  blocking collectives  81.9 us (11%)
  waiting for transfers between devices  64.1 us (8%)
  between operations  18.3 us (2%)
    scatter-add x2, other arithmetic, body(): bus_terms.at[:, :, target].add(-flow_scaled).at[:, :, column_bus]  269 us
    gather x1, local copies, waits for them, and re-layouts, body(): dispatch_value = jnp.take(network, column_bus, axis=2) + direction_capacity  181 us
    psum x1, blocking collectives, body(): lax.psum((squares_local, curvature_local), ('tm', 'net'))  77.1 us
    unnamed x3, waiting for transfers between devices  64.1 us
    scatter-add x1, other arithmetic, body(): jnp.zeros(network.shape, jnp.float32).at[:, :, anchor].add(flow_scaled)  42.8 us
    gather x1, local copies, waits for them, and re-layouts, body(): jnp.take(network, target, axis=2)  34.3 us
    gather x1, local copies, waits for them, and re-layouts, body(): jnp.take(network, anchor, axis=2) - jnp.take(network, target, axis=2)  34.3 us
  transfers between devices with their start and end apart: 4, of which 1 were waited for; matrix products, arithmetic and copies ran while one was open for 77% of the time, Pallas kernels for 0%

profile of v1, /device:TPU:1, one launch (start us, length us, event | category | flops | bytes accessed | tf_op | source)
XLA Modules:
  0.0 761.6 jit_solution(17253483734441213888)
XLA Ops:
  7.2 0.0 all-gather.3.cloned.1.call-start
  7.2 1.8 fusion
  9.0 0.0 all-gather.3.cloned.1.call-update
  9.0 0.0 reduce-scatter.4.cloned.1.call-start
  9.1 0.9 fusion.7
  9.9 3.3 collective-permute-start
  13.3 4.8 all-gather
  18.0 0.7 broadcast_multiply_fusion.1
  18.7 0.8 broadcast_clamp_fusion.1
  19.5 34.3 %gather_fusion.2 = f32[6144]{0:T(1024)S(1)} fusion(f32[8192]{0:T(1024)S(1)} %bitcast.73, s32[6144]{0:T(1024)S(1)} %get-tuple-element.11), kind=kCustom, calls=%fused_computation.1.clone | custom fusion | bytes 73728 | tf_op jit(solution)/shard_map/jit(_take)/gather | solution.py:42
  53.8 0.1 broadcast_clamp_fusion.2
  54.0 34.3 %gather_fusion.1 = f32[6144]{0:T(1024)S(1)} fusion(f32[8192]{0:T(1024)S(1)} %bitcast.74, s32[6144]{0:T(1024)S(1)} %get-tuple-element.13), kind=kCustom, calls=%fused_computation.clone | custom fusion | bytes 73728 | tf_op jit(solution)/shard_map/jit(_take)/gather | solution.py:42
  88.3 0.1 broadcast_clamp_fusion
  88.4 180.5 %gather_fusion = f32[32768]{0:T(1024)S(1)} fusion(f32[8192]{0:T(1024)S(1)} %bitcast.75, s32[32768]{0:T(1024)S(1)} %get-tuple-element.7), kind=kCustom, calls=%fused_computation.2 | custom fusion | bytes 393216 | tf_op jit(solution)/shard_map/jit(_take)/gather | solution.py:43
  269.0 0.1 fusion.6
  269.1 0.9 multiply_reduce_fusion.1
  270.0 42.8 %scatter_custom_fusion = f32[8192]{0:T(1024)S(1)} fusion(s32[6144]{0:T(1024)S(1)} %get-tuple-element.14, f32[6144]{0:T(1024)S(1)} %bitcast.89, f32[]{:T(128)} %constant.15.clone.1), kind=kCustom, calls=%fused_computation.34 | custom fusion | flops 6144 | bytes 32772 | tf_op jit(solution)/shard_map/scatter-add | solution.py:56
  312.9 42.9 %scatter_fusion = f32[8192]{0:T(1024)S(1)} fusion(f32[8192]{0:T(1024)S(1)} %scatter_custom_fusion, s32[6144]{0:T(1024)S(1)} %get-tuple-element.12, f32[6144]{0:T(1024)S(1)} %bitcast.84), kind=kCustom, calls=%fused_computation.4 | custom fusion | flops 6144 | bytes 98304 | tf_op jit(solution)/shard_map/scatter-add | solution.py:58
  356.0 0.6 collective-permute-start.1
  356.6 12.5 %reduce_sum.52 = f32[32768]{0:T(1024)S(1)} reduce(f32[128,1,32768]{2,1,0:T(1,128)} %all-gather.3.cloned.1.call-done, f32[]{:T(128)} %constant.15.clone.1), dimensions={0,1}, to_apply=%region_8.10 | reduce | flops 4161536 | bytes 16908292 | tf_op jit(solution)/shard_map/reduce_sum | solution.py:51
  369.1 0.9 multiply_reduce_fusion
  370.0 225.9 %scatter_fusion.1 = f32[8192]{0:T(1024)S(1)} fusion(f32[8192]{0:T(1024)S(1)} %scatter_fusion, s32[32768]{0:T(1024)S(1)} %get-tuple-element.8, f32[32768]{0:T(1024)S(1)} %bitcast.79), kind=kCustom, calls=%fused_computation.5 | custom fusion | flops 32768 | bytes 524288 | tf_op jit(solution)/shard_map/scatter-add | solution.py:58
  596.0 6.4 copy.18
  602.3 0.0 reduce-scatter.4.cloned.1.call-update
  602.4 0.6 multiply_reduce_fusion.3
  604.3 64.0 %reduce-scatter.4.cloned.1.call-done = f32[4096,1]{1,0:T(8,128)} async-done(((f32[8192,1]{1,0:T(8,128)}), f32[4096,1]{1,0:T(8,128)}) %reduce-scatter.4.cloned.1.call-update) | async-done | bytes 16400
  668.4 4.4 copy.19
  672.8 0.1 fusion.2
  672.9 0.6 multiply_reduce_fusion.2
  674.7 77.1 %all-reduce = (f32[1]{0:T(128)}, f32[1]{0:T(128)}) all-reduce(f32[1]{0:T(128)} %bitcast.2, f32[1]{0:T(128)} %bitcast.30), channel_id=1, replica_groups=mesh['tm'=128,'net'=2] {'tm','net'}, use_global_device_ids=true, to_apply=%region_2.3 | all-reduce | flops 2 | bytes 16 | tf_op jit(solution)/shard_map/psum | solution.py:74
  753.2 0.9 multiply_subtract_fusion
  754.1 0.7 multiply_subtract_fusion.1
  (38 shorter events, 0.2 us)
Async XLA Ops:
  7.2 349.4 %all-gather.3.cloned.1.call-start = ((), (), s32[]{:S(2)}) async-start(), calls=%async_computation.1 | async-start | bytes 16908288 | tf_op jit(solution)/shard_map/all_gather | solution.py:51
  9.0 659.3 %reduce-scatter.4.cloned.1.call-start = ((), (), s32[]{:S(2)}) async-start(), calls=%async_computation.2 | async-start | bytes 6291456
  9.9 345.9 %collective-permute-start = (f32[1,1,4096]{2,1,0:T(1,128)S(1)}, f32[1,1,4096]{2,1,0:T(1,128)S(1)}, u32[]{:S(2)}, u32[]{:S(2)}) collective-permute-start(f32[1,1,4096]{2,1,0:T(1,128)S(1)} %get-tuple-element.18), channel_id=1, source_target_pairs={{0,254},{2,0},{4,2},{6,4},{8,6},{10,8},{12,10},{14,12},{16,14},{18... | collective-permute-start | bytes 49160 | tf_op jit(solution)/shard_map/ppermute | solution.py:13
  19.5 34.3 %copy-start.13 = (s32[48]{0:T(128)S(1)}, s32[48]{0:T(128)}, u32[]{:S(2)}) copy-start(s32[48]{0:T(128)} %param.28) | copy-start | bytes 580
  19.5 34.3 %copy-start.10 = (s32[6144]{0:T(1024)S(1)}, s32[6144]{0:T(1024)}, u32[]{:S(2)}) copy-start(s32[6144]{0:T(1024)} %param.30) | copy-start | bytes 73732
  53.9 34.3 %copy-start.12 = (s32[256]{0:T(256)S(1)}, s32[256]{0:T(256)}, u32[]{:S(2)}) copy-start(s32[256]{0:T(256)} %param.32) | copy-start | bytes 3076
  53.9 34.3 %copy-start.4 = (s32[32768]{0:T(1024)S(1)}, s32[32768]{0:T(1024)}, u32[]{:S(2)}) copy-start(s32[32768]{0:T(1024)} %param.33) | copy-start | bytes 393220
  88.4 180.6 %copy-start.11 = (f32[1,6144]{1,0:T(1,128)S(1)}, f32[1,6144]{1,0:T(1,128)}, u32[]{:S(2)}) copy-start(f32[1,6144]{1,0:T(1,128)} %param.22) | copy-start | bytes 73732
  88.4 180.7 %copy-start.2 = (f32[1,1,32768]{2,1,0:T(1,128)S(1)}, f32[1,1,32768]{2,1,0:T(1,128)}, u32[]{:S(2)}) copy-start(f32[1,1,32768]{2,1,0:T(1,128)} %param.21) | copy-start | bytes 393220
  312.9 43.0 %copy-start.3 = (f32[1,1,2,4096]{3,2,1,0:T(2,128)S(1)}, f32[1,1,2,4096]{3,2,1,0:T(2,128)}, u32[]{:S(2)}) copy-start(f32[1,1,2,4096]{3,2,1,0:T(2,128)} %param.18) | copy-start | bytes 98308
  312.9 43.0 %copy-start.8 = (f32[4096]{0:T(1024)S(1)}, f32[4096]{0:T(1024)}, u32[]{:S(2)}) copy-start(f32[4096]{0:T(1024)} %param.27) | copy-start | bytes 49156
  312.9 43.0 %copy-start.9 = (f32[1,2,4096]{2,1,0:T(2,128)S(1)}, f32[1,2,4096]{2,1,0:T(2,128)}, u32[]{:S(2)}) copy-start(f32[1,2,4096]{2,1,0:T(2,128)} %param.24) | copy-start | bytes 98308
  355.9 13.1 %copy-start.1 = (f32[1,32768]{1,0:T(1,128)S(1)}, f32[1,32768]{1,0:T(1,128)}, u32[]{:S(2)}) copy-start(f32[1,32768]{1,0:T(1,128)} %param.26) | copy-start | bytes 393220
  355.9 13.1 %copy-start.6 = (f32[32768]{0:T(1024)S(1)}, f32[32768]{0:T(1024)}, u32[]{:S(2)}) copy-start(f32[32768]{0:T(1024)} %param.25) | copy-start | bytes 393220
  356.0 13.1 %copy-start = (f32[1,1,32768]{2,1,0:T(1,128)S(1)}, f32[1,1,32768]{2,1,0:T(1,128)}, u32[]{:S(2)}) copy-start(f32[1,1,32768]{2,1,0:T(1,128)} %param.19) | copy-start | bytes 393220
  356.0 13.1 %copy-start.7 = (f32[1,32768]{1,0:T(1,128)S(1)}, f32[1,32768]{1,0:T(1,128)}, u32[]{:S(2)}) copy-start(f32[1,32768]{1,0:T(1,128)} %param.23) | copy-start | bytes 393220
  356.0 316.8 %collective-permute-start.1 = (f32[1,1,4096]{2,1,0:T(1,128)S(1)}, f32[1,1,4096]{2,1,0:T(1,128)S(1)}, u32[]{:S(2)}, u32[]{:S(2)}) collective-permute-start(f32[1,1,4096]{2,1,0:T(1,128)S(1)} %subtract_multiply_fusion), channel_id=1, source_target_pairs={{0,2},{2,4},{4,6},{6,8},{8,10},{10,12},{12,14},{14,16},{16,18},{18... | collective-permute-start | bytes 49160 | tf_op jit(solution)/shard_map/ppermute | solution.py:13
  595.9 6.4 copy-start.5
Sparse Core Ops, SparseCore 0:
  10.4 232.9 all-gather.2
  602.5 65.8 reduce-scatter.3
